TPU v7x, 512 devices: a whole 4x4x16 slice. The times are simulated.
512 devices in a mesh: dp: 4 (over z_hi, core), tm: 8 (over z_lo), height: 16 (over x, y).
Axes of the slice: x: 4, y: 4, z: 16 (z_hi: 2, z_lo: 8; z = z_hi * 8 + z_lo), core: 2. Of those that a mesh axis runs over, the one named last changes fastest.
Arguments:
- clips: bfloat16 [4, 16, 64, 128, 128], P('dp', 'tm', 'height'), may hold values from -6 to 6
- frame_counts: int32 [4, 5], P('dp'), may hold values from 1 to 9, 16 in all within a row
- conv_first: bfloat16 [3, 3, 3, 128, 128], replicated, may hold values from -0.109375 to 0.109375
- conv_down: bfloat16 [3, 3, 3, 128, 128], replicated, may hold values from -0.109375 to 0.109375
- out_cotangent: bfloat16 [4, 8, 32, 64, 128], P('dp', 'tm', 'height'), may hold values from -6 to 6
Outputs:
- encoded: bfloat16 [4, 8, 32, 64, 128], P('dp', 'tm', 'height')
- grad_first: bfloat16 [3, 3, 3, 128, 128], P(None, None, None, 'dp')
- grad_down: bfloat16 [3, 3, 3, 128, 128], P(None, None, None, 'dp')
Inputs may be any that keep to these rules, and one draw needn't show every extreme that they name: `frame_counts`: each sequence's 5 clip lengths sum to 16; in every sequence one clip has exactly 9 frames.
All inputs are finite; a program needn't handle non-finite values.
Results may differ from a plain program's by a relative error of at most 0.0059.
Values may be sent and summed in bfloat16 or wider, within the bound.
No kernel may reach another device: no remote copies, remote signals or barrier semaphores. Data moves between devices by JAX's collectives and lax.ppermute only.
A program may use at most 64 MiB of HBM per device.

v0:
```python
import math
import jax
import jax.numpy as jnp
from jax import lax
from jax.sharding import PartitionSpec as P


def padded_2(cells, sides, width):
    for axis, dim in sides:
        count = lax.axis_size(axis)
        ends = count - 1
        head = lax.slice_in_dim(cells, 0, width, axis=dim)
        tail = lax.slice_in_dim(cells, cells.shape[dim] - width, cells.shape[dim], axis=dim)
        cells = jnp.concatenate(
            [
                lax.ppermute(tail, axis, [(i, (i + 1) % count) for i in range(ends)]),
                cells,
                lax.ppermute(head, axis, [((i + 1) % count, i) for i in range(ends)]),
            ],
            axis=dim,
        )
    return cells


def shifted(value, axis, steps):
    count = lax.axis_size(axis)
    leading, last = (max(0, -steps), min(count, count - steps))
    return lax.ppermute(value, axis, [(source, source + steps) for source in range(leading, last)])


def unfold(frame_slab, stride, pad_cols):
    padded = jnp.pad(frame_slab, ((0, 0), (0, 0), pad_cols, (0, 0)))
    out_rows = (padded.shape[1] - 3) // stride + 1
    out_cols = (padded.shape[2] - 3) // stride + 1
    pieces = []
    for tap_row in range(3):
        for tap_col in range(3):
            pieces.append(
                padded[
                    :,
                    tap_row : tap_row + stride * (out_rows - 1) + 1 : stride,
                    tap_col : tap_col + stride * (out_cols - 1) + 1 : stride,
                ]
            )
    joined = jnp.concatenate(pieces, axis=-1)
    return (joined.reshape(-1, joined.shape[-1]), (frame_slab.shape[0], out_rows, out_cols))


def conv_layer(extended, weight, tap_mask, out_frames, stride, pad_cols):
    channels_out = weight.shape[-1]
    summed = None
    for tap_time in range(3):
        frame_slab = extended[tap_time : tap_time + stride * (out_frames - 1) + 1 : stride]
        columns, shape_out = unfold(frame_slab, stride, pad_cols)
        kernel = weight[tap_time].reshape(-1, channels_out)
        tap_term = jnp.dot(columns, kernel, preferred_element_type=jnp.float32).reshape(
            shape_out + (channels_out,)
        )
        tap_term = tap_term * tap_mask[:, tap_time][:, None, None, None]
        summed = tap_term if summed is None else summed + tap_term
    return summed


def weight_grad(extended, grads, tap_mask, stride, pad_cols):
    out_frames = grads.shape[0]
    blocks = []
    for tap_time in range(3):
        frame_slab = extended[tap_time : tap_time + stride * (out_frames - 1) + 1 : stride]
        columns, shape_out = unfold(frame_slab, stride, pad_cols)
        masked = grads * tap_mask[:, tap_time].astype(jnp.bfloat16)[:, None, None, None]
        blocks.append(
            jnp.dot(
                columns.T, masked.reshape(-1, grads.shape[-1]), preferred_element_type=jnp.float32
            )
        )
    stacked = jnp.stack(blocks)
    return stacked.reshape(3, 3, 3, extended.shape[-1], grads.shape[-1])


def hidden_grad(grads_ext, weight, mask_ext):
    pieces = []
    for tap_time in range(3):
        masked = grads_ext * mask_ext[:, tap_time].astype(jnp.bfloat16)[:, None, None, None]
        kernel = jnp.transpose(weight[tap_time][::-1, ::-1], (0, 1, 3, 2))
        spread = lax.conv_general_dilated(
            masked,
            kernel,
            (1, 1),
            ((2, 0), (2, 2)),
            lhs_dilation=(2, 2),
            dimension_numbers=("NHWC", "HWIO", "NHWC"),
            preferred_element_type=jnp.float32,
        )
        pieces.append(spread[:, 1:, 1:])
    even_frames = pieces[2][:-1] + pieces[0][1:]
    odd_frames = pieces[1][1:]
    merged = jnp.stack([even_frames, odd_frames], axis=1)
    return merged.reshape((2 * even_frames.shape[0],) + even_frames.shape[1:])


def positions(counts_row, frame_index):
    starts = jnp.cumsum(counts_row) - counts_row
    latest = jnp.max(jnp.where(starts[None, :] <= frame_index[:, None], starts[None, :], 0), axis=1)
    return frame_index - latest


def tap_masks(place):
    return (place[:, None] >= (2 - jnp.arange(3, dtype=jnp.int32))[None, :]).astype(jnp.float32)


def body(clips, frame_counts, conv_first, conv_down, out_cotangent):
    frames_dev = clips.shape[1]
    rows_dev = clips.shape[2]
    columns_all = clips.shape[3]
    down_frames = frames_dev // 2
    counts_row = frame_counts[0]
    first_frame = lax.axis_index("tm") * frames_dev
    frame_index = first_frame + jnp.arange(frames_dev, dtype=jnp.int32)
    first_mask = tap_masks(positions(counts_row, frame_index))
    down_index = first_frame + 2 * jnp.arange(down_frames + 1, dtype=jnp.int32)
    mask_ext = tap_masks(positions(counts_row, down_index))
    down_mask = mask_ext[:down_frames]
    with_rows = padded_2(clips[0], (("height", 1),), 1)
    earlier = shifted(with_rows, "tm", 1)
    input_ext = jnp.concatenate([earlier, with_rows], axis=0)
    pre_act = conv_layer(input_ext, conv_first, first_mask, frames_dev, 1, (1, 1))
    hidden = jax.nn.silu(pre_act).astype(jnp.bfloat16)
    above = shifted(hidden[:, rows_dev - 1 :], "height", 1)
    hidden_rows = jnp.concatenate([above, hidden], axis=1)
    hidden_past = shifted(hidden_rows, "tm", 1)
    hidden_ext = jnp.concatenate([hidden_past, hidden_rows], axis=0)
    encoded = conv_layer(hidden_ext, conv_down, down_mask, down_frames, 2, (1, 0)).astype(
        jnp.bfloat16
    )
    cells_all = (
        lax.axis_size("dp")
        * clips.shape[0]
        * down_frames
        * lax.axis_size("tm")
        * (rows_dev // 2)
        * lax.axis_size("height")
        * (columns_all // 2)
    )
    scale = 1.0 / math.sqrt(cells_all)
    grads = (out_cotangent[0].astype(jnp.float32) * scale).astype(jnp.bfloat16)
    down_local = weight_grad(hidden_ext, grads, down_mask, 2, (1, 0))
    below = shifted(grads[:, 0:1], "height", -1)
    grads_rows = jnp.concatenate([grads, below], axis=1)
    grads_next = shifted(grads_rows, "tm", -1)
    grads_ext = jnp.concatenate([grads_rows, grads_next], axis=0)
    back_hidden = hidden_grad(grads_ext, conv_down, mask_ext).astype(jnp.bfloat16)
    sigma = jax.nn.sigmoid(pre_act)
    pre_grad = (back_hidden.astype(jnp.float32) * sigma * (1.0 + pre_act * (1.0 - sigma))).astype(
        jnp.bfloat16
    )
    first_local = weight_grad(input_ext, pre_grad, first_mask, 1, (1, 1))
    share = conv_first.shape[3] // lax.axis_size("dp")
    quarters = lax.axis_size("dp")

    def by_quarter(term):
        term = term.reshape(27, quarters, share, term.shape[-1])
        return jnp.transpose(term, (1, 0, 2, 3)).reshape(quarters, -1)

    stacked = jnp.concatenate([by_quarter(first_local), by_quarter(down_local)], axis=1)
    rows_n, frames_n = (lax.axis_size("height"), lax.axis_size("tm"))
    piece = stacked.reshape(quarters, rows_n, frames_n, -1)
    piece = lax.psum_scatter(piece, "height", scatter_dimension=1, tiled=True)
    piece = lax.psum_scatter(piece, "tm", scatter_dimension=2, tiled=True)
    piece = lax.psum_scatter(piece, "dp", scatter_dimension=0, tiled=True)
    piece = piece.astype(jnp.bfloat16)
    piece = lax.all_gather(piece, "tm", axis=2, tiled=True)
    gathered = lax.all_gather(piece, "height", axis=1, tiled=True).reshape(-1)
    half = gathered.shape[0] // 2
    kernel_shape = (3, 3, 3, share, conv_first.shape[-1])
    summed_first = gathered[:half].reshape(kernel_shape)
    summed_down = gathered[half:].reshape(kernel_shape)
    return (encoded[None], summed_first, summed_down)


def solution(mesh):
    in_specs = (
        P("dp", "tm", "height", None, None),
        P("dp", None),
        P(),
        P(),
        P("dp", "tm", "height", None, None),
    )
    out_specs = (
        P("dp", "tm", "height", None, None),
        P(None, None, None, "dp", None),
        P(None, None, None, "dp", None),
    )
    return jax.shard_map(body, mesh=mesh, in_specs=in_specs, out_specs=out_specs, check_vma=False)
```

profile of v0, /device:TPU:32, one launch (start us, length us, event | category | flops | bytes accessed | tf_op | source)
XLA Modules:
  0.0 460.8 jit_solution(5492218654866860973)
XLA Ops:
  7.2 0.9 fusion.92
  8.1 3.5 collective-permute-start
  11.6 1.3 collective-permute-start.1
  12.9 0.8 fusion.60
  13.7 1.3 collective-permute-start.5
  15.0 0.8 reduce-window_clone.1
  16.9 1.2 fusion.89
  21.7 5.2 %collective-permute-start.6 = (bf16[1,3,64,128]{3,2,1,0:T(8,128)(2,1)S(1)}, bf16[1,3,64,128]{3,2,1,0:T(8,128)(2,1)S(1)}, u32[]{:S(2)}, u32[]{:S(2)}) collective-permute-start(bf16[1,3,64,128]{3,2,1,0:T(8,128)(2,1)S(1)} %pad_maximum_fusion.8), channel_id=1, source_target_pairs={{16,0},{32,16},{48,32},{64,48},{80,64},{96,80},{112,96},{17,1},{33... | collective-permute-start | bytes 147464 | tf_op jit(solution)/shard_map/ppermute | solution.py:28
  27.0 2.1 collective-permute-start.2
  29.2 1.3 multiply_bitcast_fusion.1
  33.1 3.8 collective-permute-done.2
  37.9 0.8 convolution_multiply_fusion.1
  39.6 0.8 fusion.1
  40.4 0.9 fusion.10
  41.3 0.9 convolution_bitcast_fusion.5
  42.2 0.9 convolution_bitcast_fusion.4
  43.0 0.9 convolution_bitcast_fusion.3
  43.9 5.2 %collective-permute-start.3 = (bf16[2,1,128,128]{3,2,1,0:T(8,128)(2,1)S(1)}, bf16[2,1,128,128]{3,2,1,0:T(8,128)(2,1)S(1)}, u32[]{:S(2)}, u32[]{:S(2)}) collective-permute-start(bf16[2,1,128,128]{3,2,1,0:T(8,128)(2,1)S(1)} %slice.447), channel_id=1, source_target_pairs={{0,1},{1,2},{2,3},{3,4},{4,5},{5,6},{6,7},{7,8},{8,9},{9,10},{10,1... | collective-permute-start | bytes 196616 | tf_op jit(solution)/shard_map/ppermute | solution.py:28
  49.2 1.4 copy.96
  50.6 1.9 concatenate.66
  53.9 3.2 collective-permute-start.4
  57.5 5.3 %collective-permute-done.4 = bf16[2,5,128,128]{3,2,1,0:T(8,128)(2,1)S(1)} collective-permute-done((bf16[2,5,128,128]{3,2,1,0:T(8,128)(2,1)S(1)}, bf16[2,5,128,128]{3,2,1,0:T(8,128)(2,1)S(1)}, u32[]{:S(2)}, u32[]{:S(2)}) %collective-permute-start.4) | collective-permute-done | bytes 327712 | tf_op jit(solution)/shard_map/ppermute | solution.py:28
  67.7 0.8 slice.406
  72.2 0.8 constant_dynamic-update-slice_fusion.17
  73.0 0.8 constant_dynamic-update-slice_fusion.16
  74.5 0.8 constant_dynamic-update-slice_fusion.14
  76.8 0.8 constant_dynamic-update-slice_fusion.11
  78.6 0.8 constant_dynamic-update-slice_fusion.8
  79.4 0.8 constant_dynamic-update-slice_fusion.7
  80.7 1.4 copy.95
  82.1 2.9 concatenate.67
  85.0 3.6 pad_maximum_fusion
  88.7 1.3 dynamic-slice
  90.0 1.3 dynamic-slice.2
  91.3 1.3 dynamic-slice.4
  92.7 0.8 convolution_multiply_fusion.5
  93.5 132.0 %all-reduce.12.cloned.1.call-done = f32[4,16,8,1728]{3,2,1,0:T(8,128)} async-done(((f32[4,16,8,1728]{3,2,1,0:T(8,128)}), f32[4,16,8,1728]{3,2,1,0:T(8,128)}) %all-reduce.12.cloned.1.call-update) | async-done | bytes 3538960
  225.5 1.6 constant_dynamic-slice_fusion.1
  227.1 0.8 copy.71
  227.9 0.9 fusion.6
  228.8 1.4 fusion.8
  230.2 112.4 %all-reduce.14.cloned.1.call-done = f32[4,1,8,1728]{3,0,1,2:T(4,128)} async-done(((f32[4,1,8,1728]{3,0,1,2:T(4,128)}), f32[4,1,8,1728]{3,0,1,2:T(4,128)}) %all-reduce.14.cloned.1.call-update) | async-done | bytes 221200
  342.6 1.4 constant_dynamic-slice_fusion
  344.0 35.2 %all-reduce.8 = bf16[4,1,1,1728]{3,2,1,0:T(2,128)(2,1)S(1)} all-reduce(f32[4,1,1,1728]{3,2,1,0:T(1,128)S(1)} %copy.72), channel_id=4, replica_groups=mesh['dp'=4,'tm'=8,'height'=16] {'dp'}, use_global_device_ids=true, to_apply=%region_5.6.clone | all-reduce | flops 6912 | bytes 41472
  379.9 48.0 %all_gather.6 = bf16[1,1,8,1728]{3,1,0,2:T(2,128)(2,1)S(1)} all-gather(bf16[1,1,1,1728]{3,1,0,2:T(2,128)(2,1)S(1)} %fusion.64), channel_id=1, replica_groups=mesh['dp'=4,'tm'=8,'height'=16] {'tm'}, dimensions={2}, use_global_device_ids=true | all-gather | bytes 31104 | tf_op jit(solution)/shard_map/all_gather | solution.py:171
  427.9 24.0 %all_gather.7 = bf16[1,16,8,1728]{3,2,0,1:T(8,128)(2,1)S(1)} all-gather(bf16[1,1,8,1728]{3,2,0,1:T(8,128)(2,1)S(1)} %copy.74), channel_id=1, replica_groups=mesh['dp'=4,'tm'=8,'height'=16] {'height'}, dimensions={1}, use_global_device_ids=true | all-gather | bytes 470016 | tf_op jit(solution)/shard_map/all_gather | solution.py:172
  451.9 1.0 reshape.211
  452.9 1.0 reshape.212
  (150 shorter events, 22.0 us)
Async XLA Ops:
  7.2 19.8 %copy-start = (bf16[1,2,4,128,128]{4,3,2,1,0:T(8,128)(2,1)S(1)}, bf16[1,2,4,128,128]{4,3,2,1,0:T(8,128)(2,1)}, u32[]{:S(2)}) copy-start(bf16[1,2,4,128,128]{4,3,2,1,0:T(8,128)(2,1)} %param.5) | copy-start | bytes 786436
  7.2 218.3 %all-reduce.12.cloned.1.call-start = ((), (), s32[]{:S(2)}) async-start(), calls=%async_computation | async-start | bytes 7340032
  8.1 18.8 %collective-permute-start = (bf16[2,1,128,128]{3,2,1,0:T(8,128)(2,1)S(1)}, bf16[2,1,128,128]{3,2,1,0:T(8,128)(2,1)S(1)}, u32[]{:S(2)}, u32[]{:S(2)}) collective-permute-start(bf16[2,1,128,128]{3,2,1,0:T(8,128)(2,1)S(1)} %get-tuple-element.17), channel_id=1, source_target_pairs={{0,1},{1,2},{2,3},{3,4},{4,5},{5,6},{6,7},{7,8},{8,9},{9,10},{10,1... | collective-permute-start | bytes 196616 | tf_op jit(solution)/shard_map/ppermute | solution.py:16
  11.6 15.3 %collective-permute-start.1 = (bf16[2,1,128,128]{3,2,1,0:T(8,128)(2,1)S(1)}, bf16[2,1,128,128]{3,2,1,0:T(8,128)(2,1)S(1)}, u32[]{:S(2)}, u32[]{:S(2)}) collective-permute-start(bf16[2,1,128,128]{3,2,1,0:T(8,128)(2,1)S(1)} %get-tuple-element.18), channel_id=1, source_target_pairs={{1,0},{2,1},{3,2},{4,3},{5,4},{6,5},{7,6},{8,7},{9,8},{10,9},{11,1... | collective-permute-start | bytes 196616 | tf_op jit(solution)/shard_map/ppermute | solution.py:18
  13.7 8.0 %collective-permute-start.5 = (bf16[1,1,64,128]{3,2,1,0:T(8,128)(2,1)S(1)}, bf16[1,1,64,128]{3,2,1,0:T(8,128)(2,1)S(1)}, u32[]{:S(2)}, u32[]{:S(2)}) collective-permute-start(bf16[1,1,64,128]{3,2,1,0:T(8,128)(2,1)S(1)} %slice.452), channel_id=1, source_target_pairs={{1,0},{2,1},{3,2},{4,3},{5,4},{6,5},{7,6},{8,7},{9,8},{10,9},{11,1... | collective-permute-start | bytes 49160 | tf_op jit(solution)/shard_map/ppermute | solution.py:28
  21.7 7.5 %collective-permute-start.6 = (bf16[1,3,64,128]{3,2,1,0:T(8,128)(2,1)S(1)}, bf16[1,3,64,128]{3,2,1,0:T(8,128)(2,1)S(1)}, u32[]{:S(2)}, u32[]{:S(2)}) collective-permute-start(bf16[1,3,64,128]{3,2,1,0:T(8,128)(2,1)S(1)} %pad_maximum_fusion.8), channel_id=1, source_target_pairs={{16,0},{32,16},{48,32},{64,48},{80,64},{96,80},{112,96},{17,1},{33... | collective-permute-start | bytes 147464 | tf_op jit(solution)/shard_map/ppermute | solution.py:28
  27.0 4.3 copy-start.1
  27.0 4.3 copy-start.4
  27.0 9.8 %collective-permute-start.2 = (bf16[2,6,128,128]{3,2,1,0:T(8,128)(2,1)S(1)}, bf16[2,6,128,128]{3,2,1,0:T(8,128)(2,1)S(1)}, u32[]{:S(2)}, u32[]{:S(2)}) collective-permute-start(bf16[2,6,128,128]{3,2,1,0:T(8,128)(2,1)S(1)} %pad_maximum_fusion.4), channel_id=1, source_target_pairs={{0,16},{16,32},{32,48},{48,64},{64,80},{80,96},{96,112},{1,17},{17... | collective-permute-start | bytes 1179656 | tf_op jit(solution)/shard_map/ppermute | solution.py:28
  43.9 8.6 %collective-permute-start.3 = (bf16[2,1,128,128]{3,2,1,0:T(8,128)(2,1)S(1)}, bf16[2,1,128,128]{3,2,1,0:T(8,128)(2,1)S(1)}, u32[]{:S(2)}, u32[]{:S(2)}) collective-permute-start(bf16[2,1,128,128]{3,2,1,0:T(8,128)(2,1)S(1)} %slice.447), channel_id=1, source_target_pairs={{0,1},{1,2},{2,3},{3,4},{4,5},{5,6},{6,7},{7,8},{8,9},{9,10},{10,1... | collective-permute-start | bytes 196616 | tf_op jit(solution)/shard_map/ppermute | solution.py:28
  50.6 6.6 %copy-start.3 = (bf16[1,1,2,64,128]{4,3,2,1,0:T(8,128)(2,1)S(1)}, bf16[1,1,2,64,128]{4,3,2,1,0:T(8,128)(2,1)}, u32[]{:S(2)}) copy-start(bf16[1,1,2,64,128]{4,3,2,1,0:T(8,128)(2,1)} %param.9) | copy-start | bytes 98308
  53.9 9.0 %collective-permute-start.4 = (bf16[2,5,128,128]{3,2,1,0:T(8,128)(2,1)S(1)}, bf16[2,5,128,128]{3,2,1,0:T(8,128)(2,1)S(1)}, u32[]{:S(2)}, u32[]{:S(2)}) collective-permute-start(bf16[2,5,128,128]{3,2,1,0:T(8,128)(2,1)S(1)} %pad_maximum_fusion.3), channel_id=1, source_target_pairs={{0,16},{16,32},{32,48},{48,64},{64,80},{80,96},{96,112},{1,17},{17... | collective-permute-start | bytes 983048 | tf_op jit(solution)/shard_map/ppermute | solution.py:28
  88.6 3.9 copy-start.2
  88.7 253.9 %all-reduce.14.cloned.1.call-start = ((), (), s32[]{:S(2)}) async-start(), calls=%async_computation.1 | async-start | bytes 458752
Sparse Core Ops, SparseCore 0:
  88.8 136.6 all-reduce.11
  228.4 114.1 all-reduce.13
where the time goes:
time: 462 us; the launch traced here: 461 us
  waiting for transfers between devices  253 us (55%)
  blocking collectives  107 us (23%)
  local copies, waits for them, and re-layouts  43.2 us (9%)
  starting transfers between devices  21.8 us (5%)
  between operations  16.9 us (4%)
  matrix products  10 us (2%)
  other arithmetic  8.16 us (2%)
    unnamed x4, waiting for transfers between devices  244 us
    all_gather x1, blocking collectives, body(): piece = lax.all_gather(piece, 'tm', axis=2, tiled=True)  48 us
    unnamed x1, blocking collectives  35.2 us
    all_gather x1, blocking collectives, body(): gathered = lax.all_gather(piece, 'height', axis=1, tiled=True).reshape(-1)  24 us
    unnamed x66, local copies, waits for them, and re-layouts  17 us
    ppermute x5, starting transfers between devices, shifted(): lax.ppermute(value, axis, [(source, source + steps) for source in range(l...  17 us
    slice x27, local copies, waits for them, and re-layouts, unfold(): padded[:, tap_row:tap_row + stride * (out_rows - 1) + 1:stride, tap_col:t...  9.5 us
  transfers between devices with their start and end apart: 9, of which 4 were waited for; matrix products, arithmetic and copies ran while one was open for 4% of the time, Pallas kernels for 0%

commit v1 on v0

--- a/solution.py
+++ b/solution.py
@@ -3,6 +3,22 @@
 import jax.numpy as jnp
 from jax import lax
 from jax.sharding import PartitionSpec as P
+
+
+def gather_around(x, axis, dim):
+    ways, here, hop = (lax.axis_size(axis), lax.axis_index(axis), x.shape[dim])
+    shape = [n * ways if d == dim else n for d, n in enumerate(x.shape)]
+    full = lax.dynamic_update_slice_in_dim(jnp.zeros(shape, x.dtype), x, here * hop, axis=dim)
+    going_up = going_down = x
+    for far in range(1, ways // 2 + 1):
+        going_up = lax.ppermute(going_up, axis, [(d, (d + 1) % ways) for d in range(ways)])
+        full = lax.dynamic_update_slice_in_dim(full, going_up, (here - far) % ways * hop, axis=dim)
+        if 2 * far < ways:
+            going_down = lax.ppermute(going_down, axis, [(d, (d - 1) % ways) for d in range(ways)])
+            full = lax.dynamic_update_slice_in_dim(
+                full, going_down, (here + far) % ways * hop, axis=dim
+            )
+    return full
 
 
 def padded_2(cells, sides, width):
@@ -169,7 +185,7 @@
     piece = lax.psum_scatter(piece, "dp", scatter_dimension=0, tiled=True)
     piece = piece.astype(jnp.bfloat16)
     piece = lax.all_gather(piece, "tm", axis=2, tiled=True)
-    gathered = lax.all_gather(piece, "height", axis=1, tiled=True).reshape(-1)
+    gathered = gather_around(piece, "height", 1).reshape(-1)
     half = gathered.shape[0] // 2
     kernel_shape = (3, 3, 3, share, conv_first.shape[-1])
     summed_first = gathered[:half].reshape(kernel_shape)

time: 462 us -> 514 us (1.11)
  starting transfers between devices: 21.8 us -> 87.7 us
  blocking collectives: 107 us -> 83.2 us
  waiting for transfers between devices: 253 us -> 262 us
    ppermute x0 -> x15, starting transfers between devices: none -> 66 us  [the longest x7 49.2 us: gather_around(): lax.ppermute(going_down, axis, [(d, (d - 1) % ways) for d in range(ways)])]
    all_gather x1 -> x0, blocking collectives: 24 us -> none  [body(): gathered = lax.all_gather(piece, 'height', axis=1, tiled=True).reshape(-1)]
    ppermute x0 -> x15, waiting for transfers between devices: none -> 8.88 us  [the longest x8 8.87 us: gather_around(): lax.ppermute(going_up, axis, [(d, (d + 1) % ways) for d in range(ways)])]
  transfers between devices with their start and end apart: 9 -> 24, of which waited for: 4 -> 12; matrix products, arithmetic and copies ran while one was open for 4% -> 4% of each run, Pallas kernels for 0% -> 0%
where the time goes in v1:
time: 514 us; the launch traced here: 512 us
  waiting for transfers between devices  262 us (51%)
  starting transfers between devices  87.7 us (17%)
  blocking collectives  83.2 us (16%)
  local copies, waits for them, and re-layouts  43.3 us (8%)
  between operations  17.5 us (3%)
  matrix products  10 us (2%)
  other arithmetic  8.14 us (2%)
    unnamed x4, waiting for transfers between devices  244 us
    ppermute x7, starting transfers between devices, gather_around(): lax.ppermute(going_down, axis, [(d, (d - 1) % ways) for d in range(ways)])  49.2 us
    all_gather x1, blocking collectives, body(): piece = lax.all_gather(piece, 'tm', axis=2, tiled=True)  48 us
    unnamed x1, blocking collectives  35.2 us
    unnamed x66, local copies, waits for them, and re-layouts  16.9 us
    ppermute x5, starting transfers between devices, shifted(): lax.ppermute(value, axis, [(source, source + steps) for source in range(l...  16.8 us
    ppermute x8, starting transfers between devices, gather_around(): lax.ppermute(going_up, axis, [(d, (d + 1) % ways) for d in range(ways)])  16.8 us
  transfers between devices with their start and end apart: 24, of which 12 were waited for; matrix products, arithmetic and copies ran while one was open for 4% of the time, Pallas kernels for 0%

profile of v1, /device:TPU:32, one launch (start us, length us, event | category | flops | bytes accessed | tf_op | source)
XLA Modules:
  0.0 512.0 jit_solution(456662591205294138)
XLA Ops:
  7.2 0.9 fusion.92
  8.1 3.5 collective-permute-start
  11.6 1.3 collective-permute-start.1
  13.7 1.3 collective-permute-start.5
  16.9 1.3 fusion.89
  21.8 5.2 %collective-permute-start.6 = (bf16[1,3,64,128]{3,2,1,0:T(8,128)(2,1)S(1)}, bf16[1,3,64,128]{3,2,1,0:T(8,128)(2,1)S(1)}, u32[]{:S(2)}, u32[]{:S(2)}) collective-permute-start(bf16[1,3,64,128]{3,2,1,0:T(8,128)(2,1)S(1)} %pad_maximum_fusion.8), channel_id=1, source_target_pairs={{16,0},{32,16},{48,32},{64,48},{80,64},{96,80},{112,96},{17,1},{33... | collective-permute-start | bytes 147464 | tf_op jit(solution)/shard_map/ppermute | solution.py:44
  27.1 1.9 collective-permute-start.2
  29.2 1.3 multiply_bitcast_fusion.1
  33.0 3.8 collective-permute-done.2
  40.3 0.9 fusion.10
  42.1 0.9 convolution_bitcast_fusion.4
  43.9 5.2 %collective-permute-start.3 = (bf16[2,1,128,128]{3,2,1,0:T(8,128)(2,1)S(1)}, bf16[2,1,128,128]{3,2,1,0:T(8,128)(2,1)S(1)}, u32[]{:S(2)}, u32[]{:S(2)}) collective-permute-start(bf16[2,1,128,128]{3,2,1,0:T(8,128)(2,1)S(1)} %slice.447), channel_id=1, source_target_pairs={{0,1},{1,2},{2,3},{3,4},{4,5},{5,6},{6,7},{7,8},{8,9},{9,10},{10,1... | collective-permute-start | bytes 196616 | tf_op jit(solution)/shard_map/ppermute | solution.py:44
  49.2 1.4 copy.142
  50.6 1.9 concatenate.66
  53.8 3.2 collective-permute-start.4
  57.5 5.3 %collective-permute-done.4 = bf16[2,5,128,128]{3,2,1,0:T(8,128)(2,1)S(1)} collective-permute-done((bf16[2,5,128,128]{3,2,1,0:T(8,128)(2,1)S(1)}, bf16[2,5,128,128]{3,2,1,0:T(8,128)(2,1)S(1)}, u32[]{:S(2)}, u32[]{:S(2)}) %collective-permute-start.4) | collective-permute-done | bytes 327712 | tf_op jit(solution)/shard_map/ppermute | solution.py:44
  80.7 1.4 copy.141
  82.1 2.9 concatenate.67
  84.9 3.6 pad_maximum_fusion
  88.9 1.3 dynamic-slice
  90.1 1.3 dynamic-slice.2
  91.4 1.3 dynamic-slice.4
  93.6 131.8 %all-reduce.12.cloned.1.call-done = f32[4,16,8,1728]{3,2,1,0:T(8,128)} async-done(((f32[4,16,8,1728]{3,2,1,0:T(8,128)}), f32[4,16,8,1728]{3,2,1,0:T(8,128)}) %all-reduce.12.cloned.1.call-update) | async-done | bytes 3538960
  225.4 1.6 constant_dynamic-slice_fusion.1
  227.8 0.9 fusion.6
  228.6 1.4 fusion.8
  230.1 112.4 %all-reduce.14.cloned.1.call-done = f32[4,1,8,1728]{3,0,1,2:T(4,128)} async-done(((f32[4,1,8,1728]{3,0,1,2:T(4,128)}), f32[4,1,8,1728]{3,0,1,2:T(4,128)}) %all-reduce.14.cloned.1.call-update) | async-done | bytes 221200
  342.5 1.4 constant_dynamic-slice_fusion
  343.9 35.2 %all-reduce.8 = bf16[4,1,1,1728]{3,2,1,0:T(2,128)(2,1)S(1)} all-reduce(f32[4,1,1,1728]{3,2,1,0:T(1,128)S(1)} %copy.87), channel_id=4, replica_groups=mesh['dp'=4,'tm'=8,'height'=16] {'dp'}, use_global_device_ids=true, to_apply=%region_5.6.clone | all-reduce | flops 6912 | bytes 41472
  379.8 48.0 %all_gather.3 = bf16[1,1,8,1728]{3,1,0,2:T(2,128)(2,1)S(1)} all-gather(bf16[1,1,1,1728]{3,1,0,2:T(2,128)(2,1)S(1)} %fusion.64), channel_id=1, replica_groups=mesh['dp'=4,'tm'=8,'height'=16] {'tm'}, dimensions={2}, use_global_device_ids=true | all-gather | bytes 31104 | tf_op jit(solution)/shard_map/all_gather | solution.py:187
  427.8 3.4 collective-permute-start.7
  431.2 5.8 %collective-permute-start.8 = (bf16[1,1,8,1728]{3,1,0,2:T(2,128)(2,1)S(1)}, bf16[1,1,8,1728]{3,1,0,2:T(2,128)(2,1)S(1)}, u32[]{:S(2)}, u32[]{:S(2)}) collective-permute-start(bf16[1,1,8,1728]{3,1,0,2:T(2,128)(2,1)S(1)} %all_gather.3), channel_id=1, source_target_pairs={{0,15},{1,0},{2,1},{3,2},{4,3},{5,4},{6,5},{7,6},{8,7},{9,8},{10,9... | collective-permute-start | bytes 82952 | tf_op jit(solution)/shard_map/ppermute | solution.py:17
  437.2 1.9 collective-permute-start.9
  439.1 7.2 %collective-permute-start.10 = (bf16[1,1,8,1728]{3,1,0,2:T(2,128)(2,1)S(1)}, bf16[1,1,8,1728]{3,1,0,2:T(2,128)(2,1)S(1)}, u32[]{:S(2)}, u32[]{:S(2)}) collective-permute-start(bf16[1,1,8,1728]{3,1,0,2:T(2,128)(2,1)S(1)} %collective-permute-done.8), channel_id=1, source_target_pairs={{0,15},{1,0},{2,1},{3,2},{4,3},{5,4},{6,5},{7,6},{8,7},{9,8},{10,9... | collective-permute-start | bytes 82952 | tf_op jit(solution)/shard_map/ppermute | solution.py:17
  446.6 1.9 collective-permute-start.11
  448.5 7.2 %collective-permute-start.12 = (bf16[1,1,8,1728]{3,1,0,2:T(2,128)(2,1)S(1)}, bf16[1,1,8,1728]{3,1,0,2:T(2,128)(2,1)S(1)}, u32[]{:S(2)}, u32[]{:S(2)}) collective-permute-start(bf16[1,1,8,1728]{3,1,0,2:T(2,128)(2,1)S(1)} %collective-permute-done.10), channel_id=1, source_target_pairs={{0,15},{1,0},{2,1},{3,2},{4,3},{5,4},{6,5},{7,6},{8,7},{9,8},{10,9... | collective-permute-start | bytes 82952 | tf_op jit(solution)/shard_map/ppermute | solution.py:17
  455.9 1.9 collective-permute-start.13
  457.9 7.2 %collective-permute-start.14 = (bf16[1,1,8,1728]{3,1,0,2:T(2,128)(2,1)S(1)}, bf16[1,1,8,1728]{3,1,0,2:T(2,128)(2,1)S(1)}, u32[]{:S(2)}, u32[]{:S(2)}) collective-permute-start(bf16[1,1,8,1728]{3,1,0,2:T(2,128)(2,1)S(1)} %collective-permute-done.12), channel_id=1, source_target_pairs={{0,15},{1,0},{2,1},{3,2},{4,3},{5,4},{6,5},{7,6},{8,7},{9,8},{10,9... | collective-permute-start | bytes 82952 | tf_op jit(solution)/shard_map/ppermute | solution.py:17
  465.3 1.9 collective-permute-start.15
  467.2 7.2 %collective-permute-start.16 = (bf16[1,1,8,1728]{3,1,0,2:T(2,128)(2,1)S(1)}, bf16[1,1,8,1728]{3,1,0,2:T(2,128)(2,1)S(1)}, u32[]{:S(2)}, u32[]{:S(2)}) collective-permute-start(bf16[1,1,8,1728]{3,1,0,2:T(2,128)(2,1)S(1)} %collective-permute-done.14), channel_id=1, source_target_pairs={{0,15},{1,0},{2,1},{3,2},{4,3},{5,4},{6,5},{7,6},{8,7},{9,8},{10,9... | collective-permute-start | bytes 82952 | tf_op jit(solution)/shard_map/ppermute | solution.py:17
  474.7 1.9 collective-permute-start.17
  476.6 7.2 %collective-permute-start.18 = (bf16[1,1,8,1728]{3,1,0,2:T(2,128)(2,1)S(1)}, bf16[1,1,8,1728]{3,1,0,2:T(2,128)(2,1)S(1)}, u32[]{:S(2)}, u32[]{:S(2)}) collective-permute-start(bf16[1,1,8,1728]{3,1,0,2:T(2,128)(2,1)S(1)} %collective-permute-done.16), channel_id=1, source_target_pairs={{0,15},{1,0},{2,1},{3,2},{4,3},{5,4},{6,5},{7,6},{8,7},{9,8},{10,9... | collective-permute-start | bytes 82952 | tf_op jit(solution)/shard_map/ppermute | solution.py:17
  484.4 1.9 collective-permute-start.19
  486.3 7.2 %collective-permute-start.20 = (bf16[1,1,8,1728]{3,1,0,2:T(2,128)(2,1)S(1)}, bf16[1,1,8,1728]{3,1,0,2:T(2,128)(2,1)S(1)}, u32[]{:S(2)}, u32[]{:S(2)}) collective-permute-start(bf16[1,1,8,1728]{3,1,0,2:T(2,128)(2,1)S(1)} %collective-permute-done.18), channel_id=1, source_target_pairs={{0,15},{1,0},{2,1},{3,2},{4,3},{5,4},{6,5},{7,6},{8,7},{9,8},{10,9... | collective-permute-start | bytes 82952 | tf_op jit(solution)/shard_map/ppermute | solution.py:17
  493.8 1.9 collective-permute-start.21
  495.7 7.4 %collective-permute-done.21 = bf16[1,1,8,1728]{3,1,0,2:T(2,128)(2,1)S(1)} collective-permute-done((bf16[1,1,8,1728]{3,1,0,2:T(2,128)(2,1)S(1)}, bf16[1,1,8,1728]{3,1,0,2:T(2,128)(2,1)S(1)}, u32[]{:S(2)}, u32[]{:S(2)}) %collective-permute-start.21) | collective-permute-done | bytes 27680 | tf_op jit(solution)/shard_map/ppermute | solution.py:14
  503.2 1.0 reshape.211
  504.2 1.0 reshape.212
  (195 shorter events, 35.6 us)
Async XLA Ops:
  7.2 19.9 %copy-start = (bf16[1,2,4,128,128]{4,3,2,1,0:T(8,128)(2,1)S(1)}, bf16[1,2,4,128,128]{4,3,2,1,0:T(8,128)(2,1)}, u32[]{:S(2)}) copy-start(bf16[1,2,4,128,128]{4,3,2,1,0:T(8,128)(2,1)} %param.5) | copy-start | bytes 786436
  7.2 218.2 %all-reduce.12.cloned.1.call-start = ((), (), s32[]{:S(2)}) async-start(), calls=%async_computation | async-start | bytes 7340032
  8.1 18.9 %collective-permute-start = (bf16[2,1,128,128]{3,2,1,0:T(8,128)(2,1)S(1)}, bf16[2,1,128,128]{3,2,1,0:T(8,128)(2,1)S(1)}, u32[]{:S(2)}, u32[]{:S(2)}) collective-permute-start(bf16[2,1,128,128]{3,2,1,0:T(8,128)(2,1)S(1)} %get-tuple-element.17), channel_id=1, source_target_pairs={{0,1},{1,2},{2,3},{3,4},{4,5},{5,6},{6,7},{7,8},{8,9},{9,10},{10,1... | collective-permute-start | bytes 196616 | tf_op jit(solution)/shard_map/ppermute | solution.py:32
  11.6 15.4 %collective-permute-start.1 = (bf16[2,1,128,128]{3,2,1,0:T(8,128)(2,1)S(1)}, bf16[2,1,128,128]{3,2,1,0:T(8,128)(2,1)S(1)}, u32[]{:S(2)}, u32[]{:S(2)}) collective-permute-start(bf16[2,1,128,128]{3,2,1,0:T(8,128)(2,1)S(1)} %get-tuple-element.18), channel_id=1, source_target_pairs={{1,0},{2,1},{3,2},{4,3},{5,4},{6,5},{7,6},{8,7},{9,8},{10,9},{11,1... | collective-permute-start | bytes 196616 | tf_op jit(solution)/shard_map/ppermute | solution.py:34
  13.7 8.1 %collective-permute-start.5 = (bf16[1,1,64,128]{3,2,1,0:T(8,128)(2,1)S(1)}, bf16[1,1,64,128]{3,2,1,0:T(8,128)(2,1)S(1)}, u32[]{:S(2)}, u32[]{:S(2)}) collective-permute-start(bf16[1,1,64,128]{3,2,1,0:T(8,128)(2,1)S(1)} %slice.452), channel_id=1, source_target_pairs={{1,0},{2,1},{3,2},{4,3},{5,4},{6,5},{7,6},{8,7},{9,8},{10,9},{11,1... | collective-permute-start | bytes 49160 | tf_op jit(solution)/shard_map/ppermute | solution.py:44
  16.9 14.0 %copy-start.1 = (bf16[3,3,3,128,128]{4,3,2,1,0:T(8,128)(2,1)S(1)}, bf16[3,3,3,128,128]{4,3,2,1,0:T(8,128)(2,1)}, u32[]{:S(2)}) copy-start(bf16[3,3,3,128,128]{4,3,2,1,0:T(8,128)(2,1)} %param.8) | copy-start | bytes 2654212
  16.9 14.0 %copy-start.4 = (pred[8,18]{0,1:T(8,128)(4,1)S(1)}, pred[8,18]{0,1:T(8,128)(4,1)}, u32[]{:S(2)}) copy-start(pred[8,18]{0,1:T(8,128)(4,1)} %constant.154) | copy-start | bytes 436
  21.8 7.3 %collective-permute-start.6 = (bf16[1,3,64,128]{3,2,1,0:T(8,128)(2,1)S(1)}, bf16[1,3,64,128]{3,2,1,0:T(8,128)(2,1)S(1)}, u32[]{:S(2)}, u32[]{:S(2)}) collective-permute-start(bf16[1,3,64,128]{3,2,1,0:T(8,128)(2,1)S(1)} %pad_maximum_fusion.8), channel_id=1, source_target_pairs={{16,0},{32,16},{48,32},{64,48},{80,64},{96,80},{112,96},{17,1},{33... | collective-permute-start | bytes 147464 | tf_op jit(solution)/shard_map/ppermute | solution.py:44
  27.1 9.7 %collective-permute-start.2 = (bf16[2,6,128,128]{3,2,1,0:T(8,128)(2,1)S(1)}, bf16[2,6,128,128]{3,2,1,0:T(8,128)(2,1)S(1)}, u32[]{:S(2)}, u32[]{:S(2)}) collective-permute-start(bf16[2,6,128,128]{3,2,1,0:T(8,128)(2,1)S(1)} %pad_maximum_fusion.4), channel_id=1, source_target_pairs={{0,16},{16,32},{32,48},{48,64},{64,80},{80,96},{96,112},{1,17},{17... | collective-permute-start | bytes 1179656 | tf_op jit(solution)/shard_map/ppermute | solution.py:44
  43.9 8.6 %collective-permute-start.3 = (bf16[2,1,128,128]{3,2,1,0:T(8,128)(2,1)S(1)}, bf16[2,1,128,128]{3,2,1,0:T(8,128)(2,1)S(1)}, u32[]{:S(2)}, u32[]{:S(2)}) collective-permute-start(bf16[2,1,128,128]{3,2,1,0:T(8,128)(2,1)S(1)} %slice.447), channel_id=1, source_target_pairs={{0,1},{1,2},{2,3},{3,4},{4,5},{5,6},{6,7},{7,8},{8,9},{9,10},{10,1... | collective-permute-start | bytes 196616 | tf_op jit(solution)/shard_map/ppermute | solution.py:44
  50.6 6.6 %copy-start.3 = (bf16[1,1,2,64,128]{4,3,2,1,0:T(8,128)(2,1)S(1)}, bf16[1,1,2,64,128]{4,3,2,1,0:T(8,128)(2,1)}, u32[]{:S(2)}) copy-start(bf16[1,1,2,64,128]{4,3,2,1,0:T(8,128)(2,1)} %param.9) | copy-start | bytes 98308
  53.8 9.0 %collective-permute-start.4 = (bf16[2,5,128,128]{3,2,1,0:T(8,128)(2,1)S(1)}, bf16[2,5,128,128]{3,2,1,0:T(8,128)(2,1)S(1)}, u32[]{:S(2)}, u32[]{:S(2)}) collective-permute-start(bf16[2,5,128,128]{3,2,1,0:T(8,128)(2,1)S(1)} %pad_maximum_fusion.3), channel_id=1, source_target_pairs={{0,16},{16,32},{32,48},{48,64},{64,80},{80,96},{96,112},{1,17},{17... | collective-permute-start | bytes 983048 | tf_op jit(solution)/shard_map/ppermute | solution.py:44
  88.6 4.1 copy-start.2
  88.6 253.9 %all-reduce.14.cloned.1.call-start = ((), (), s32[]{:S(2)}) async-start(), calls=%async_computation.1 | async-start | bytes 458752
  427.8 9.4 %collective-permute-start.7 = (bf16[1,1,8,1728]{3,1,0,2:T(2,128)(2,1)S(1)}, bf16[1,1,8,1728]{3,1,0,2:T(2,128)(2,1)S(1)}, u32[]{:S(2)}, u32[]{:S(2)}) collective-permute-start(bf16[1,1,8,1728]{3,1,0,2:T(2,128)(2,1)S(1)} %all_gather.3), channel_id=1, source_target_pairs={{0,1},{1,2},{2,3},{3,4},{4,5},{5,6},{6,7},{7,8},{8,9},{9,10},{10,1... | collective-permute-start | bytes 82952 | tf_op jit(solution)/shard_map/ppermute | solution.py:14
  431.2 7.9 %collective-permute-start.8 = (bf16[1,1,8,1728]{3,1,0,2:T(2,128)(2,1)S(1)}, bf16[1,1,8,1728]{3,1,0,2:T(2,128)(2,1)S(1)}, u32[]{:S(2)}, u32[]{:S(2)}) collective-permute-start(bf16[1,1,8,1728]{3,1,0,2:T(2,128)(2,1)S(1)} %all_gather.3), channel_id=1, source_target_pairs={{0,15},{1,0},{2,1},{3,2},{4,3},{5,4},{6,5},{7,6},{8,7},{9,8},{10,9... | collective-permute-start | bytes 82952 | tf_op jit(solution)/shard_map/ppermute | solution.py:17
  437.2 9.4 %collective-permute-start.9 = (bf16[1,1,8,1728]{3,1,0,2:T(2,128)(2,1)S(1)}, bf16[1,1,8,1728]{3,1,0,2:T(2,128)(2,1)S(1)}, u32[]{:S(2)}, u32[]{:S(2)}) collective-permute-start(bf16[1,1,8,1728]{3,1,0,2:T(2,128)(2,1)S(1)} %collective-permute-done.7), channel_id=1, source_target_pairs={{0,1},{1,2},{2,3},{3,4},{4,5},{5,6},{6,7},{7,8},{8,9},{9,10},{10,1... | collective-permute-start | bytes 82952 | tf_op jit(solution)/shard_map/ppermute | solution.py:14
  439.1 9.4 %collective-permute-start.10 = (bf16[1,1,8,1728]{3,1,0,2:T(2,128)(2,1)S(1)}, bf16[1,1,8,1728]{3,1,0,2:T(2,128)(2,1)S(1)}, u32[]{:S(2)}, u32[]{:S(2)}) collective-permute-start(bf16[1,1,8,1728]{3,1,0,2:T(2,128)(2,1)S(1)} %collective-permute-done.8), channel_id=1, source_target_pairs={{0,15},{1,0},{2,1},{3,2},{4,3},{5,4},{6,5},{7,6},{8,7},{9,8},{10,9... | collective-permute-start | bytes 82952 | tf_op jit(solution)/shard_map/ppermute | solution.py:17
  446.6 9.4 %collective-permute-start.11 = (bf16[1,1,8,1728]{3,1,0,2:T(2,128)(2,1)S(1)}, bf16[1,1,8,1728]{3,1,0,2:T(2,128)(2,1)S(1)}, u32[]{:S(2)}, u32[]{:S(2)}) collective-permute-start(bf16[1,1,8,1728]{3,1,0,2:T(2,128)(2,1)S(1)} %collective-permute-done.9), channel_id=1, source_target_pairs={{0,1},{1,2},{2,3},{3,4},{4,5},{5,6},{6,7},{7,8},{8,9},{9,10},{10,1... | collective-permute-start | bytes 82952 | tf_op jit(solution)/shard_map/ppermute | solution.py:14
  448.5 9.4 %collective-permute-start.12 = (bf16[1,1,8,1728]{3,1,0,2:T(2,128)(2,1)S(1)}, bf16[1,1,8,1728]{3,1,0,2:T(2,128)(2,1)S(1)}, u32[]{:S(2)}, u32[]{:S(2)}) collective-permute-start(bf16[1,1,8,1728]{3,1,0,2:T(2,128)(2,1)S(1)} %collective-permute-done.10), channel_id=1, source_target_pairs={{0,15},{1,0},{2,1},{3,2},{4,3},{5,4},{6,5},{7,6},{8,7},{9,8},{10,9... | collective-permute-start | bytes 82952 | tf_op jit(solution)/shard_map/ppermute | solution.py:17
  455.9 9.4 %collective-permute-start.13 = (bf16[1,1,8,1728]{3,1,0,2:T(2,128)(2,1)S(1)}, bf16[1,1,8,1728]{3,1,0,2:T(2,128)(2,1)S(1)}, u32[]{:S(2)}, u32[]{:S(2)}) collective-permute-start(bf16[1,1,8,1728]{3,1,0,2:T(2,128)(2,1)S(1)} %collective-permute-done.11), channel_id=1, source_target_pairs={{0,1},{1,2},{2,3},{3,4},{4,5},{5,6},{6,7},{7,8},{8,9},{9,10},{10,1... | collective-permute-start | bytes 82952 | tf_op jit(solution)/shard_map/ppermute | solution.py:14
  457.9 9.4 %collective-permute-start.14 = (bf16[1,1,8,1728]{3,1,0,2:T(2,128)(2,1)S(1)}, bf16[1,1,8,1728]{3,1,0,2:T(2,128)(2,1)S(1)}, u32[]{:S(2)}, u32[]{:S(2)}) collective-permute-start(bf16[1,1,8,1728]{3,1,0,2:T(2,128)(2,1)S(1)} %collective-permute-done.12), channel_id=1, source_target_pairs={{0,15},{1,0},{2,1},{3,2},{4,3},{5,4},{6,5},{7,6},{8,7},{9,8},{10,9... | collective-permute-start | bytes 82952 | tf_op jit(solution)/shard_map/ppermute | solution.py:17
  465.3 9.4 %collective-permute-start.15 = (bf16[1,1,8,1728]{3,1,0,2:T(2,128)(2,1)S(1)}, bf16[1,1,8,1728]{3,1,0,2:T(2,128)(2,1)S(1)}, u32[]{:S(2)}, u32[]{:S(2)}) collective-permute-start(bf16[1,1,8,1728]{3,1,0,2:T(2,128)(2,1)S(1)} %collective-permute-done.13), channel_id=1, source_target_pairs={{0,1},{1,2},{2,3},{3,4},{4,5},{5,6},{6,7},{7,8},{8,9},{9,10},{10,1... | collective-permute-start | bytes 82952 | tf_op jit(solution)/shard_map/ppermute | solution.py:14
  467.2 9.4 %collective-permute-start.16 = (bf16[1,1,8,1728]{3,1,0,2:T(2,128)(2,1)S(1)}, bf16[1,1,8,1728]{3,1,0,2:T(2,128)(2,1)S(1)}, u32[]{:S(2)}, u32[]{:S(2)}) collective-permute-start(bf16[1,1,8,1728]{3,1,0,2:T(2,128)(2,1)S(1)} %collective-permute-done.14), channel_id=1, source_target_pairs={{0,15},{1,0},{2,1},{3,2},{4,3},{5,4},{6,5},{7,6},{8,7},{9,8},{10,9... | collective-permute-start | bytes 82952 | tf_op jit(solution)/shard_map/ppermute | solution.py:17
  474.7 9.7 %collective-permute-start.17 = (bf16[1,1,8,1728]{3,1,0,2:T(2,128)(2,1)S(1)}, bf16[1,1,8,1728]{3,1,0,2:T(2,128)(2,1)S(1)}, u32[]{:S(2)}, u32[]{:S(2)}) collective-permute-start(bf16[1,1,8,1728]{3,1,0,2:T(2,128)(2,1)S(1)} %collective-permute-done.15), channel_id=1, source_target_pairs={{0,1},{1,2},{2,3},{3,4},{4,5},{5,6},{6,7},{7,8},{8,9},{9,10},{10,1... | collective-permute-start | bytes 82952 | tf_op jit(solution)/shard_map/ppermute | solution.py:14
  476.6 9.7 %collective-permute-start.18 = (bf16[1,1,8,1728]{3,1,0,2:T(2,128)(2,1)S(1)}, bf16[1,1,8,1728]{3,1,0,2:T(2,128)(2,1)S(1)}, u32[]{:S(2)}, u32[]{:S(2)}) collective-permute-start(bf16[1,1,8,1728]{3,1,0,2:T(2,128)(2,1)S(1)} %collective-permute-done.16), channel_id=1, source_target_pairs={{0,15},{1,0},{2,1},{3,2},{4,3},{5,4},{6,5},{7,6},{8,7},{9,8},{10,9... | collective-permute-start | bytes 82952 | tf_op jit(solution)/shard_map/ppermute | solution.py:17
  484.4 9.4 %collective-permute-start.19 = (bf16[1,1,8,1728]{3,1,0,2:T(2,128)(2,1)S(1)}, bf16[1,1,8,1728]{3,1,0,2:T(2,128)(2,1)S(1)}, u32[]{:S(2)}, u32[]{:S(2)}) collective-permute-start(bf16[1,1,8,1728]{3,1,0,2:T(2,128)(2,1)S(1)} %collective-permute-done.17), channel_id=1, source_target_pairs={{0,1},{1,2},{2,3},{3,4},{4,5},{5,6},{6,7},{7,8},{8,9},{9,10},{10,1... | collective-permute-start | bytes 82952 | tf_op jit(solution)/shard_map/ppermute | solution.py:14
  486.3 9.4 %collective-permute-start.20 = (bf16[1,1,8,1728]{3,1,0,2:T(2,128)(2,1)S(1)}, bf16[1,1,8,1728]{3,1,0,2:T(2,128)(2,1)S(1)}, u32[]{:S(2)}, u32[]{:S(2)}) collective-permute-start(bf16[1,1,8,1728]{3,1,0,2:T(2,128)(2,1)S(1)} %collective-permute-done.18), channel_id=1, source_target_pairs={{0,15},{1,0},{2,1},{3,2},{4,3},{5,4},{6,5},{7,6},{8,7},{9,8},{10,9... | collective-permute-start | bytes 82952 | tf_op jit(solution)/shard_map/ppermute | solution.py:17
  493.8 9.4 %collective-permute-start.21 = (bf16[1,1,8,1728]{3,1,0,2:T(2,128)(2,1)S(1)}, bf16[1,1,8,1728]{3,1,0,2:T(2,128)(2,1)S(1)}, u32[]{:S(2)}, u32[]{:S(2)}) collective-permute-start(bf16[1,1,8,1728]{3,1,0,2:T(2,128)(2,1)S(1)} %collective-permute-done.19), channel_id=1, source_target_pairs={{0,1},{1,2},{2,3},{3,4},{4,5},{5,6},{6,7},{7,8},{8,9},{9,10},{10,1... | collective-permute-start | bytes 82952 | tf_op jit(solution)/shard_map/ppermute | solution.py:14
Sparse Core Ops, SparseCore 0:
  88.7 136.6 all-reduce.11
  228.3 114.1 all-reduce.13
